TPU v7x, 512 devices: a whole 4x4x16 slice. The times are simulated.
512 devices in a mesh: ctx: 64 (over z, x_hi, core), head: 8 (over y, x_lo).
Axes of the slice: x: 4 (x_hi: 2, x_lo: 2; x = x_hi * 2 + x_lo), y: 4, z: 16, core: 2. Of those that a mesh axis runs over, the one named last changes fastest.
Arguments:
- tokens: bfloat16 [8192, 4096], P('ctx'), may hold values from -6 to 6
- norm_gain: float32 [4096], replicated, may hold values from 0.25 to 1.75
- w_query: bfloat16 [4096, 4096], P('ctx', 'head'), may hold values from -0.09375 to 0.09375
- w_key: bfloat16 [4096, 1024], P('ctx', 'head'), may hold values from -0.09375 to 0.09375
- w_value: bfloat16 [4096, 1024], P('ctx', 'head'), may hold values from -0.09375 to 0.09375
- w_out: bfloat16 [4096, 4096], P('head', 'ctx'), may hold values from -0.09375 to 0.09375
- row_map: int32 [8192], P('ctx'), may hold values from 0 to 8191, as said below
- doc_lengths: int32 [32], replicated, may hold values from 1 to 2048, 8192 in all
- doc_labels: int32 [32], replicated, may hold values from 0 to 1, as said below
Outputs:
- residual_out: bfloat16 [8192, 4096], P('ctx', 'head')
- refusal_direction: float32 [4096], P('head')
Inputs may be any that keep to these rules, and one draw needn't show every extreme that they name: `row_map`: the rows of ctx index c are two runs of 64 consecutive positions, run b(c) and run 2 * 64 - 1 - b(c) of the pack, b a permutation drawn from the seed; every position appears once. `doc_labels`: at least one prompt of each class.
All inputs are finite; a program needn't handle non-finite values.
Results may differ from a plain program's by a relative error of at most 0.008.
Values may be sent and summed in bfloat16 or wider, within the bound.
No kernel may reach another device: no remote copies, remote signals or barrier semaphores. Data moves between devices by JAX's collectives and lax.ppermute only.
A program may use at most 64 MiB of HBM per device.

v0:
```python
import math
import jax
import jax.numpy as jnp
from jax import lax
from jax.sharding import Mesh
from jax.sharding import PartitionSpec as P

HEADS = 32
KV_HEADS = 8
HEAD_DIM = 128
MOST = 2048
RUN = 64
ROPE_BASE = 500000.0
NEG_FILL = -1e30
CTX = ("z", "xh", "c")
HEAD = ("y", "xl")


def doc_layout(row_map, doc_lengths):
    doc_ends = jnp.cumsum(doc_lengths)
    doc_starts = doc_ends - doc_lengths
    doc_index = jnp.sum((row_map[:, None] >= doc_ends[None, :]).astype(jnp.int32), 1)
    member = doc_index[:, None] == jnp.arange(doc_ends.shape[0], dtype=jnp.int32)[None, :]
    in_doc = row_map - jnp.sum(jnp.where(member, doc_starts[None, :], 0), 1)
    return (doc_index, in_doc, doc_ends)


def rotate(values, in_doc):
    head_dim = values.shape[-1]
    half_dim = head_dim // 2
    inv_freq = jnp.exp(
        jnp.arange(half_dim).astype(jnp.float32) * (-2.0 * math.log(ROPE_BASE) / head_dim)
    )
    angles = in_doc.astype(jnp.float32)[:, None] * inv_freq[None, :]
    shape_out = (angles.shape[0],) + (1,) * (values.ndim - 2) + (half_dim,)
    cosine = jnp.cos(angles).reshape(shape_out)
    sine_val = jnp.sin(angles).reshape(shape_out)
    front_half = values[..., :half_dim]
    back_half = values[..., half_dim:]
    return jnp.concatenate(
        [front_half * cosine - back_half * sine_val, back_half * cosine + front_half * sine_val], -1
    )


def rms_norm(tokens, norm_gain):
    wide_tokens = tokens.astype(jnp.float32)
    row_scale = lax.rsqrt(jnp.mean(wide_tokens * wide_tokens, -1, keepdims=True) + 1e-05)
    return (wide_tokens * row_scale * norm_gain).astype(jnp.bfloat16)


def swap_cat(x, axis_name):
    return jnp.concatenate([x, lax.ppermute(x, axis_name, [(0, 1), (1, 0)])], 0)


def gather_z(x):
    return lax.all_gather(x, "z", axis=0, tiled=True)


def gather_pair(x):
    return swap_cat(swap_cat(x, "xh"), "c")


def relative_index():
    return (
        lax.axis_index("c") ^ jnp.arange(2, dtype=jnp.int32),
        lax.axis_index("xh") ^ jnp.arange(2, dtype=jnp.int32),
    )


def to_gathered_order(x, sizes):
    nz, nxh, nc = sizes
    c_idx, xh_idx = relative_index()
    y = jnp.transpose(x.reshape(x.shape[0], nz, nxh, nc, x.shape[-1]), (0, 3, 2, 1, 4))
    y = jnp.take(jnp.take(y, c_idx, axis=1), xh_idx, axis=2)
    return y.reshape(x.shape)


def from_gathered_order(x, sizes):
    nz, nxh, nc = sizes
    c_idx, xh_idx = relative_index()
    y = x.reshape(x.shape[0], nc, nxh, nz, x.shape[-1])
    y = jnp.take(jnp.take(y, c_idx, axis=1), xh_idx, axis=2)
    return jnp.transpose(y, (0, 3, 2, 1, 4)).reshape(x.shape)


def reduce_scatter_head(x, head_sizes):
    ny, nxl = head_sizes
    rows, width = x.shape
    xl = lax.axis_index("xl")
    y = lax.axis_index("y")
    grouped = x.reshape(rows, ny, nxl, width // (ny * nxl))
    kept = jnp.take(grouped, xl, axis=2)
    sent = jnp.take(grouped, (xl + 1) % nxl, axis=2).astype(jnp.bfloat16)
    summed = kept + lax.ppermute(sent, "xl", [(0, 1), (1, 0)]).astype(jnp.float32)
    acc = jnp.take(summed, y, axis=1)
    for shift in range(1, ny):
        piece = jnp.take(summed, (y + shift) % ny, axis=1).astype(jnp.bfloat16)
        acc = acc + lax.ppermute(piece, "y", [(i, (i + shift) % ny) for i in range(ny)]).astype(
            jnp.float32
        )
    return acc


def make_local(sizes, head_sizes):
    nz, nxh, nc = sizes
    nctx = nz * nxh * nc

    def local(tokens, norm_gain, w_query, w_key, w_value, w_out, row_map, doc_lengths, doc_labels):
        tok_rows, width = tokens.shape
        d_rows = w_query.shape[0]
        q_cols = w_query.shape[1]
        kv_cols = w_key.shape[1]
        group_size = q_cols // kv_cols
        runs_here = tok_rows // RUN
        total_runs = runs_here * nctx
        win_runs = MOST // RUN + 1
        normed = rms_norm(tokens, norm_gain)
        doc_index, in_doc, doc_ends = doc_layout(row_map, doc_lengths)
        qkv_cols = q_cols + 2 * kv_cols
        out_cols = w_out.shape[0]
        w_z = gather_z(jnp.concatenate([w_query, w_key, w_value, w_out.T], axis=1))
        w_o = gather_pair(w_z[:, qkv_cols:]).reshape(nctx, d_rows, out_cols)
        w_proj = w_z[:, :qkv_cols]
        pair = ("xh", "c")
        npair = nxh * nc
        me = lax.axis_index("xh") * nc + lax.axis_index("c")
        quarters = jnp.transpose(
            normed.reshape(tok_rows, nz, nxh, nc, d_rows), (0, 2, 3, 1, 4)
        ).reshape(tok_rows, npair, nz * d_rows)
        perms = [[(i, i ^ flip) for i in range(npair)] for flip in range(1, npair)]
        theirs = [
            lax.ppermute(jnp.take(quarters, me ^ flip, axis=1), pair, perm)
            for flip, perm in zip(range(1, npair), perms)
        ]
        stacked = jnp.concatenate([jnp.take(quarters, me, axis=1)] + theirs, axis=0)
        parts = jnp.dot(stacked, w_proj, preferred_element_type=jnp.float32)
        rows = tok_rows
        on_chip = lax.ppermute(
            jnp.concatenate([parts[rows : 2 * rows], parts[3 * rows : 4 * rows]]), pair, perms[0]
        )
        across = lax.ppermute(parts[2 * rows : 3 * rows] + on_chip[rows:], pair, perms[1])
        proj = parts[:rows] + on_chip[:rows] + across
        queries = proj[:, :q_cols].reshape(tok_rows, group_size, HEAD_DIM)
        key_proj = proj[:, q_cols : q_cols + kv_cols]
        value_proj = proj[:, q_cols + kv_cols :].astype(jnp.bfloat16)
        queries = rotate(queries, in_doc).astype(jnp.bfloat16)
        key_proj = rotate(key_proj, in_doc).astype(jnp.bfloat16)
        assert 2 * tok_rows == 2 * kv_cols
        pos_row = jnp.concatenate([row_map // RUN, row_map % RUN]).astype(jnp.bfloat16)[None, :]
        kv_buf = jnp.concatenate(
            [jnp.concatenate([key_proj, value_proj], axis=1), jnp.pad(pos_row, ((0, 7), (0, 0)))],
            axis=0,
        )
        kv = gather_pair(gather_z(kv_buf)).reshape(nctx, tok_rows + 8, 2 * kv_cols)
        pos_code = kv[:, tok_rows, :].astype(jnp.int32)
        key_pos_all = pos_code[:, :tok_rows] * RUN + pos_code[:, tok_rows:]
        kv_halves = kv[:, :tok_rows].reshape(total_runs, RUN, 2 * kv_cols)
        pos_halves = key_pos_all.reshape(total_runs, RUN)
        run_of_half = pos_halves[:, 0] // RUN
        half_of_run = (
            jnp.zeros((total_runs,), jnp.int32)
            .at[run_of_half]
            .set(jnp.arange(total_runs, dtype=jnp.int32))
        )
        q_pos = row_map.reshape(runs_here, RUN)
        q_start = (row_map - in_doc).reshape(runs_here, RUN)
        q_run = q_pos[:, 0] // RUN
        first_run = jnp.maximum(q_run - (win_runs - 1), 0)
        win = first_run[:, None] + jnp.arange(win_runs, dtype=jnp.int32)[None, :]
        win_halves = half_of_run[win]
        kv_win = kv_halves[win_halves].reshape(runs_here, win_runs * RUN, 2 * kv_cols)
        k_pos = pos_halves[win_halves].reshape(runs_here, win_runs * RUN)
        k_win = kv_win[..., :kv_cols]
        v_win = kv_win[..., kv_cols:]
        q_runs = queries.reshape(runs_here, RUN, group_size, HEAD_DIM)
        scale_factor = HEAD_DIM ** (-0.5)
        scores = (
            jnp.einsum("rqgd,rkd->rgqk", q_runs, k_win, preferred_element_type=jnp.float32)
            * scale_factor
        )
        allowed = (k_pos[:, None, :] >= q_start[:, :, None]) & (
            k_pos[:, None, :] <= q_pos[:, :, None]
        )
        allowed = allowed[:, None]
        scores = jnp.where(allowed, scores, NEG_FILL)
        row_top = jnp.max(scores, -1, keepdims=True)
        weights = jnp.where(allowed, jnp.exp(scores - row_top), 0.0)
        row_sum = jnp.sum(weights, -1, keepdims=True)
        mixed = (
            jnp.einsum(
                "rgqk,rkd->rgqd",
                weights.astype(jnp.bfloat16),
                v_win,
                preferred_element_type=jnp.float32,
            )
            / row_sum
        ).astype(jnp.bfloat16)
        attended = jnp.transpose(mixed, (0, 2, 1, 3)).reshape(tok_rows, q_cols)
        partial_g = jnp.einsum("tk,jdk->tjd", attended, w_o, preferred_element_type=jnp.float32)
        partial_out = from_gathered_order(partial_g, sizes).reshape(tok_rows, width)
        head_share = reduce_scatter_head(partial_out, head_sizes)
        col_width = head_share.shape[1]
        head_idx = lax.axis_index("y") * head_sizes[1] + lax.axis_index("xl")
        own_cols = lax.dynamic_slice_in_dim(tokens, head_idx * col_width, col_width, 1)
        residual_out = (own_cols.astype(jnp.float32) + head_share).astype(jnp.bfloat16)
        is_last = row_map[:, None] == (doc_ends - 1)[None, :]
        label_f = doc_labels.astype(jnp.float32)
        harmful = jnp.sum(label_f)
        harmless = doc_labels.shape[0] - jnp.sum(label_f)
        stream = residual_out.astype(jnp.float32)
        harm_rows = jnp.sum(jnp.where(is_last, label_f[None, :], 0.0), 1)
        safe_rows = jnp.sum(jnp.where(is_last, (1.0 - label_f)[None, :], 0.0), 1)
        sums = jnp.stack(
            [jnp.sum(harm_rows[:, None] * stream, 0), jnp.sum(safe_rows[:, None] * stream, 0)]
        )
        for axis in (("xh", "c"), "z"):
            sums = lax.psum(sums, axis)
        refusal_direction = sums[0] / harmful - sums[1] / harmless
        return (residual_out, refusal_direction)

    return local


def solution(mesh):
    n_ctx = mesh.shape["ctx"]
    n_head = mesh.shape["head"]
    nc, nxh = (2, 2)
    nz = n_ctx // (nc * nxh)
    ny, nxl = (n_head // 2, 2)
    fine = Mesh(mesh.devices.reshape(nz, nxh, nc, ny, nxl), ("z", "xh", "c", "y", "xl"))
    placed = (
        P(CTX, None),
        P(),
        P(CTX, HEAD),
        P(CTX, HEAD),
        P(CTX, HEAD),
        P(HEAD, CTX),
        P(CTX),
        P(),
        P(),
    )
    return jax.shard_map(
        make_local((nz, nxh, nc), (ny, nxl)),
        mesh=fine,
        in_specs=placed,
        out_specs=(P(CTX, HEAD), P(HEAD)),
        check_vma=False,
    )
```

profile of v0, /device:TPU:8, one launch (start us, length us, event | category | flops | bytes accessed | tf_op | source)
XLA Modules:
  0.0 339.4 jit_solution(16196009366355087545)
XLA Ops:
  7.2 1.6 pad_maximum_fusion.5
  8.9 1.6 copy.85
  12.1 1.9 collective-permute-start
  14.0 4.9 %collective-permute-start.1 = (bf16[128,1024]{0,1:T(8,128)(2,1)S(1)}, bf16[128,1024]{0,1:T(8,128)(2,1)S(1)}, u32[]{:S(2)}, u32[]{:S(2)}) collective-permute-start(bf16[128,1024]{0,1:T(8,128)(2,1)S(1)} %get-tuple-element.60), channel_id=1, source_target_pairs={{0,16},{8,24},{16,0},{24,8},{1,17},{9,25},{17,1},{25,9},{2,18},{10... | collective-permute-start | bytes 786440 | tf_op jit(solution)/shard_map/ppermute | solution.py:132
  18.9 2.2 collective-permute-start.2
  21.2 5.3 %collective-permute-done.1 = bf16[128,1024]{0,1:T(8,128)(2,1)S(1)} collective-permute-done((bf16[128,1024]{0,1:T(8,128)(2,1)S(1)}, bf16[128,1024]{0,1:T(8,128)(2,1)S(1)}, u32[]{:S(2)}, u32[]{:S(2)}) %collective-permute-start.1) | collective-permute-done | bytes 262176 | tf_op jit(solution)/shard_map/ppermute | solution.py:132
  26.5 4.9 %collective-permute-done.2 = bf16[128,1024]{0,1:T(8,128)(2,1)} collective-permute-done((bf16[128,1024]{0,1:T(8,128)(2,1)S(1)}, bf16[128,1024]{0,1:T(8,128)(2,1)}, u32[]{:S(2)}, u32[]{:S(2)}) %collective-permute-start.2) | collective-permute-done | bytes 262176 | tf_op jit(solution)/shard_map/ppermute | solution.py:132
  31.4 58.0 %all-gather.3.cloned.1.call-done = bf16[1024,1280]{1,0:T(8,128)(2,1)} async-done(((bf16[64,1280]{1,0:T(8,128)(2,1)}), bf16[1024,1280]{1,0:T(8,128)(2,1)}) %all-gather.3.cloned.1.call-update) | async-done | bytes 2621456 | tf_op jit(solution)/shard_map/all_gather | solution.py:56
  89.5 2.5 fusion.11
  92.1 1.9 collective-permute-start.3
  95.0 1.4 collective-permute-done.3
  96.4 1.1 slice_add_fusion
  97.5 4.9 %collective-permute-start.4 = (f32[128,768]{0,1:T(8,128)S(1)}, f32[128,768]{0,1:T(8,128)S(1)}, u32[]{:S(2)}, u32[]{:S(2)}) collective-permute-start(f32[128,768]{0,1:T(8,128)S(1)} %slice_add_fusion), channel_id=1, source_target_pairs={{0,16},{8,24},{16,0},{24,8},{1,17},{9,25},{17,1},{25,9},{2,18},{10... | collective-permute-start | bytes 1179656 | tf_op jit(solution)/shard_map/ppermute | solution.py:141
  102.6 9.5 %collective-permute-done.4 = f32[128,768]{0,1:T(8,128)S(1)} collective-permute-done((f32[128,768]{0,1:T(8,128)S(1)}, f32[128,768]{0,1:T(8,128)S(1)}, u32[]{:S(2)}, u32[]{:S(2)}) %collective-permute-start.4) | collective-permute-done | bytes 393248 | tf_op jit(solution)/shard_map/ppermute | solution.py:141
  112.1 1.1 fusion.31
  115.5 1.3 slice.159
  116.8 4.9 %collective-permute-start.7 = (bf16[1024,512]{1,0:T(8,128)(2,1)S(1)}, bf16[1024,512]{1,0:T(8,128)(2,1)}, u32[]{:S(2)}, u32[]{:S(2)}) collective-permute-start(bf16[1024,512]{1,0:T(8,128)(2,1)S(1)} %slice.159), channel_id=1, source_target_pairs={{0,16},{16,0},{1,17},{17,1},{2,18},{18,2},{3,19},{19,3},{4,20},{20... | collective-permute-start | bytes 3145736 | tf_op jit(solution)/shard_map/ppermute | solution.py:52
  121.7 62.2 %all-gather.5.cloned.1.call-done = bf16[2176,256]{1,0:T(8,128)(2,1)} async-done(((bf16[136,256]{1,0:T(8,128)(2,1)}), bf16[2176,256]{1,0:T(8,128)(2,1)}) %all-gather.5.cloned.1.call-update) | async-done | bytes 1114128 | tf_op jit(solution)/shard_map/all_gather | solution.py:56
  183.9 4.9 %collective-permute-start.5 = (bf16[2176,256]{1,0:T(8,128)(2,1)}, bf16[2176,256]{1,0:T(8,128)(2,1)S(1)}, u32[]{:S(2)}, u32[]{:S(2)}) collective-permute-start(bf16[2176,256]{1,0:T(8,128)(2,1)} %all-gather.5.cloned.1.call-done), channel_id=1, source_target_pairs={{0,16},{16,0},{1,17},{17,1},{2,18},{18,2},{3,19},{19,3},{4,20},{20... | collective-permute-start | bytes 3342344 | tf_op jit(solution)/shard_map/ppermute | solution.py:52
  188.8 2.7 pad_maximum_fusion.3
  191.5 2.0 collective-permute-start.8
  193.6 11.2 %collective-permute-done.5 = bf16[2176,256]{1,0:T(8,128)(2,1)S(1)} collective-permute-done((bf16[2176,256]{1,0:T(8,128)(2,1)}, bf16[2176,256]{1,0:T(8,128)(2,1)S(1)}, u32[]{:S(2)}, u32[]{:S(2)}) %collective-permute-start.5) | collective-permute-done | bytes 1114144 | tf_op jit(solution)/shard_map/ppermute | solution.py:52
  204.7 1.7 pad_maximum_fusion.2
  206.5 1.9 collective-permute-start.6
  210.2 1.4 subtract_convert_fusion
  214.3 3.6 %pad_maximum_fusion.1 = bf16[4096,512]{1,0:T(8,128)(2,1)} fusion(bf16[2048,512]{1,0:T(8,128)(2,1)} %collective-permute-done.8, bf16[1024,512]{1,0:T(8,128)(2,1)} %collective-permute-done.7, bf16[1024,512]{1,0:T(8,128)(2,1)S(1)} %slice.159), kind=kLoop, calls=%fused_computation.14 | loop fusion | flops 12582912 | bytes 8388608 | tf_op jit(solution)/shard_map/concatenate | solution.py:52
  217.9 11.3 %pad_maximum_fusion = bf16[8704,256]{1,0:T(8,128)(2,1)S(1)} fusion(bf16[4352,256]{1,0:T(8,128)(2,1)} %collective-permute-done.6, bf16[2176,256]{1,0:T(8,128)(2,1)S(1)} %copy-done.2, bf16[2176,256]{1,0:T(8,128)(2,1)S(1)} %copy-done), kind=kLoop, calls=%fused_computation.13 | loop fusion | flops 13369344 | bytes 8912896 | tf_op jit(solution)/shard_map/concatenate | solution.py:52
  229.2 2.5 slice.153
  232.0 1.2 scatter_custom_fusion
  233.2 1.2 gather_fusion
  235.2 2.9 gather_fusion.2
  238.5 4.5 %fusion.63 = (f32[2,4,64]{2,1,0:T(4,128)S(1)}, bf16[2,4,64,2112]{3,2,1,0:T(8,128)(2,1)}) fusion(pred[2,64,2112]{2,1,0:T(8,128)(4,1)S(1)} %compare_and_fusion, bf16[2,2112,256]{2,1,0:T(8,128)(2,1)S(1)} %bitcast.117, bf16[2,64,4,64]{3,1,2,0:T(8,128)(2,1)} %copy.98, bf16[2,64,4,64]{3,1,2,0:T(8,128)(2,1)} %copy.97), kind=kOutput, calls=%fused_computation.145 | convolution fusion | flops 283576384 | bytes 3934208 | tf_op jit(solution)/shard_map/sub | solution.py:187
  243.0 2.4 fusion.19
  245.6 3.4 %fusion.40 = f32[128,2,2,16,64]{0,4,3,2,1:T(8,128)S(1)} fusion(bf16[2,2,16,64,512]{4,3,2,1,0:T(8,128)(2,1)} %bitcast.111, bf16[128,512,1,1,1]{1,0,2,3,4:T(8,128)(2,1)S(1)} %reshape.594), kind=kOutput, calls=%fused_computation.71 | convolution fusion | flops 536870912 | bytes 6422528 | tf_op jit(solution)/shard_map/tk,jdk->tjd/dot_general | solution.py:199
  249.0 2.0 gather_fusion.3
  251.0 3.3 select_bitcast_fusion.1
  254.4 2.3 gather_fusion.4
  258.1 2.8 collective-permute-start.9
  261.0 13.6 %collective-permute-done.9 = bf16[128,4,512]{0,2,1:T(8,128)(2,1)} collective-permute-done((bf16[128,4,512]{0,2,1:T(8,128)(2,1)}, bf16[128,4,512]{0,2,1:T(8,128)(2,1)}, u32[]{:S(2)}, u32[]{:S(2)}) %collective-permute-start.9) | collective-permute-done | bytes 524320 | tf_op jit(solution)/shard_map/ppermute | solution.py:94
  274.7 1.1 fusion.30
  276.9 3.4 collective-permute-start.10
  280.3 3.1 collective-permute-start.11
  283.3 4.0 %collective-permute-start.12 = (bf16[128,512]{0,1:T(8,128)(2,1)S(1)}, bf16[128,512]{0,1:T(8,128)(2,1)S(1)}, u32[]{:S(2)}, u32[]{:S(2)}) collective-permute-start(bf16[128,512]{0,1:T(8,128)(2,1)S(1)} %get-tuple-element.56), channel_id=1, source_target_pairs={{0,6},{2,0},{4,2},{6,4},{1,7},{3,1},{5,3},{7,5},{8,14},{10,8},{12,... | collective-permute-start | bytes 393224 | tf_op jit(solution)/shard_map/ppermute | solution.py:98
  289.7 1.6 collective-permute-done.12
  291.3 1.2 fusion.32
  292.5 8.5 %psum.14 = f32[2,512]{1,0:T(2,128)S(1)} all-reduce(f32[2,512]{1,0:T(2,128)S(1)} %pad_maximum_fusion.12), channel_id=1, replica_groups=mesh['z'=16,'xh'=2,'c'=2,'y'=4,'xl'=2] {'xh','c'}, use_global_device_ids=true, to_apply=%region_11.15 | all-reduce | flops 1024 | bytes 8192 | tf_op jit(solution)/shard_map/psum | solution.py:217
  301.0 29.5 %psum.15 = f32[2,512]{1,0:T(2,128)S(1)} all-reduce(f32[2,512]{1,0:T(2,128)S(1)} %psum.14), channel_id=1, replica_groups=mesh['z'=16,'xh'=2,'c'=2,'y'=4,'xl'=2] {'z'}, use_global_device_ids=true, to_apply=%region_12.16 | all-reduce | flops 1024 | bytes 8192 | tf_op jit(solution)/shard_map/psum | solution.py:217
  331.3 1.3 divide_subtract_fusion
  (99 shorter events, 16.1 us)
Async XLA Ops:
  7.2 4.0 %copy-start.5 = (f32[4096]{0:T(1024)S(1)}, f32[4096]{0:T(1024)}, u32[]{:S(2)}) copy-start(f32[4096]{0:T(1024)} %param.16) | copy-start | bytes 49156
  7.2 82.3 %all-gather.3.cloned.1.call-start = ((), (), s32[]{:S(2)}) async-start(), calls=%async_computation | async-start | bytes 2785280 | tf_op jit(solution)/shard_map/all_gather | solution.py:56
  8.8 175.0 %all-gather.5.cloned.1.call-start = ((), (), s32[]{:S(2)}) async-start(), calls=%async_computation.1 | async-start | bytes 1183744 | tf_op jit(solution)/shard_map/all_gather | solution.py:56
  12.1 9.1 %collective-permute-start = (bf16[128,1024]{0,1:T(8,128)(2,1)S(1)}, bf16[128,1024]{0,1:T(8,128)(2,1)S(1)}, u32[]{:S(2)}, u32[]{:S(2)}) collective-permute-start(bf16[128,1024]{0,1:T(8,128)(2,1)S(1)} %get-tuple-element.61), channel_id=1, source_target_pairs={{0,8},{8,0},{16,24},{24,16},{1,9},{9,1},{17,25},{25,17},{2,10},{10... | collective-permute-start | bytes 786440 | tf_op jit(solution)/shard_map/ppermute | solution.py:132
  14.0 12.5 %collective-permute-start.1 = (bf16[128,1024]{0,1:T(8,128)(2,1)S(1)}, bf16[128,1024]{0,1:T(8,128)(2,1)S(1)}, u32[]{:S(2)}, u32[]{:S(2)}) collective-permute-start(bf16[128,1024]{0,1:T(8,128)(2,1)S(1)} %get-tuple-element.60), channel_id=1, source_target_pairs={{0,16},{8,24},{16,0},{24,8},{1,17},{9,25},{17,1},{25,9},{2,18},{10... | collective-permute-start | bytes 786440 | tf_op jit(solution)/shard_map/ppermute | solution.py:132
  18.9 12.5 %collective-permute-start.2 = (bf16[128,1024]{0,1:T(8,128)(2,1)S(1)}, bf16[128,1024]{0,1:T(8,128)(2,1)}, u32[]{:S(2)}, u32[]{:S(2)}) collective-permute-start(bf16[128,1024]{0,1:T(8,128)(2,1)S(1)} %get-tuple-element.59), channel_id=1, source_target_pairs={{0,24},{8,16},{16,8},{24,0},{1,25},{9,17},{17,9},{25,1},{2,26},{10... | collective-permute-start | bytes 786440 | tf_op jit(solution)/shard_map/ppermute | solution.py:132
  92.0 2.1 copy-start.8
  92.0 2.3 copy-start.9
  92.1 4.3 %collective-permute-start.3 = (f32[256,768]{0,1:T(8,128)S(1)}, f32[256,768]{0,1:T(8,128)}, u32[]{:S(2)}, u32[]{:S(2)}) collective-permute-start(f32[256,768]{0,1:T(8,128)S(1)} %pad_maximum_fusion.4), channel_id=1, source_target_pairs={{0,8},{8,0},{16,24},{24,16},{1,9},{9,1},{17,25},{25,17},{2,10},{10... | collective-permute-start | bytes 2359304 | tf_op jit(solution)/shard_map/ppermute | solution.py:138
  97.5 14.6 %collective-permute-start.4 = (f32[128,768]{0,1:T(8,128)S(1)}, f32[128,768]{0,1:T(8,128)S(1)}, u32[]{:S(2)}, u32[]{:S(2)}) collective-permute-start(f32[128,768]{0,1:T(8,128)S(1)} %slice_add_fusion), channel_id=1, source_target_pairs={{0,16},{8,24},{16,0},{24,8},{1,17},{9,25},{17,1},{25,9},{2,18},{10... | collective-permute-start | bytes 1179656 | tf_op jit(solution)/shard_map/ppermute | solution.py:141
  113.1 0.8 copy-start.4
  116.8 72.0 %collective-permute-start.7 = (bf16[1024,512]{1,0:T(8,128)(2,1)S(1)}, bf16[1024,512]{1,0:T(8,128)(2,1)}, u32[]{:S(2)}, u32[]{:S(2)}) collective-permute-start(bf16[1024,512]{1,0:T(8,128)(2,1)S(1)} %slice.159), channel_id=1, source_target_pairs={{0,16},{16,0},{1,17},{17,1},{2,18},{18,2},{3,19},{19,3},{4,20},{20... | collective-permute-start | bytes 3145736 | tf_op jit(solution)/shard_map/ppermute | solution.py:52
  183.9 20.9 %copy-start = (bf16[2176,256]{1,0:T(8,128)(2,1)S(1)}, bf16[2176,256]{1,0:T(8,128)(2,1)}, u32[]{:S(2)}) copy-start(bf16[2176,256]{1,0:T(8,128)(2,1)} %all-gather.5.cloned.1.call-done) | copy-start | bytes 3342340
  183.9 20.8 %collective-permute-start.5 = (bf16[2176,256]{1,0:T(8,128)(2,1)}, bf16[2176,256]{1,0:T(8,128)(2,1)S(1)}, u32[]{:S(2)}, u32[]{:S(2)}) collective-permute-start(bf16[2176,256]{1,0:T(8,128)(2,1)} %all-gather.5.cloned.1.call-done), channel_id=1, source_target_pairs={{0,16},{16,0},{1,17},{17,1},{2,18},{18,2},{3,19},{19,3},{4,20},{20... | collective-permute-start | bytes 3342344 | tf_op jit(solution)/shard_map/ppermute | solution.py:52
  191.5 18.7 %slice-start = ((f32[128,768]{0,1:T(8,128)}), f32[128,512]{0,1:T(8,128)S(1)}, s32[]{:S(2)}) async-start(f32[128,768]{0,1:T(8,128)} %copy-done.4), calls=%async_computation.2 | async-start | bytes 524288 | tf_op jit(solution)/shard_map/slice | solution.py:143
  191.5 22.8 %collective-permute-start.8 = (bf16[2048,512]{1,0:T(8,128)(2,1)}, bf16[2048,512]{1,0:T(8,128)(2,1)}, u32[]{:S(2)}, u32[]{:S(2)}) collective-permute-start(bf16[2048,512]{1,0:T(8,128)(2,1)} %pad_maximum_fusion.3), channel_id=1, source_target_pairs={{0,8},{8,0},{1,9},{9,1},{2,10},{10,2},{3,11},{11,3},{4,12},{12,4},... | collective-permute-start | bytes 6291464 | tf_op jit(solution)/shard_map/ppermute | solution.py:52
  204.7 1.8 copy-start.1
  206.5 11.4 %collective-permute-start.6 = (bf16[4352,256]{1,0:T(8,128)(2,1)}, bf16[4352,256]{1,0:T(8,128)(2,1)}, u32[]{:S(2)}, u32[]{:S(2)}) collective-permute-start(bf16[4352,256]{1,0:T(8,128)(2,1)} %pad_maximum_fusion.2), channel_id=1, source_target_pairs={{0,8},{8,0},{1,9},{9,1},{2,10},{10,2},{3,11},{11,3},{4,12},{12,4},... | collective-permute-start | bytes 6684680 | tf_op jit(solution)/shard_map/ppermute | solution.py:52
  214.3 3.6 %copy-start.2 = (bf16[2176,256]{1,0:T(8,128)(2,1)S(1)}, bf16[2176,256]{1,0:T(8,128)(2,1)}, u32[]{:S(2)}) copy-start(bf16[2176,256]{1,0:T(8,128)(2,1)} %copy-done.1) | copy-start | bytes 3342340
  235.2 3.0 copy-start.12
  249.0 2.0 copy-start.7
  254.4 2.3 copy-start.6
  257.2 30.1 %copy-start.13 = (s32[32]{0:T(128)S(1)}, s32[32]{0:T(128)}, u32[]{:S(2)}) copy-start(s32[32]{0:T(128)} %param.23) | copy-start | bytes 388
  257.2 31.5 %copy-start.10 = (s32[128]{0:T(128)S(1)}, s32[128]{0:T(128)}, u32[]{:S(2)}) copy-start(s32[128]{0:T(128)} %param.21) | copy-start | bytes 1540
  257.2 31.5 %copy-start.11 = (s32[32]{0:T(128)S(1)}, s32[32]{0:T(128)}, u32[]{:S(2)}) copy-start(s32[32]{0:T(128)} %get-tuple-element.76) | copy-start | bytes 388
  258.1 16.5 %collective-permute-start.9 = (bf16[128,4,512]{0,2,1:T(8,128)(2,1)}, bf16[128,4,512]{0,2,1:T(8,128)(2,1)}, u32[]{:S(2)}, u32[]{:S(2)}) collective-permute-start(bf16[128,4,512]{0,2,1:T(8,128)(2,1)} %bitcast_convert_fusion), channel_id=1, source_target_pairs={{0,1},{1,0},{2,3},{3,2},{4,5},{5,4},{6,7},{7,6},{8,9},{9,8},{10,11... | collective-permute-start | bytes 1572872 | tf_op jit(solution)/shard_map/ppermute | solution.py:94
  275.8 1.0 copy-start.3
  276.9 12.0 %collective-permute-start.10 = (bf16[128,512]{0,1:T(8,128)(2,1)S(1)}, bf16[128,512]{0,1:T(8,128)(2,1)S(1)}, u32[]{:S(2)}, u32[]{:S(2)}) collective-permute-start(bf16[128,512]{0,1:T(8,128)(2,1)S(1)} %get-tuple-element.55), channel_id=1, source_target_pairs={{0,2},{2,4},{4,6},{6,0},{1,3},{3,5},{5,7},{7,1},{8,10},{10,12},{12... | collective-permute-start | bytes 393224 | tf_op jit(solution)/shard_map/ppermute | solution.py:98
  280.3 9.5 %collective-permute-start.11 = (bf16[128,512]{0,1:T(8,128)(2,1)S(1)}, bf16[128,512]{0,1:T(8,128)(2,1)S(1)}, u32[]{:S(2)}, u32[]{:S(2)}) collective-permute-start(bf16[128,512]{0,1:T(8,128)(2,1)S(1)} %get-tuple-element.57), channel_id=1, source_target_pairs={{0,4},{2,6},{4,0},{6,2},{1,5},{3,7},{5,1},{7,3},{8,12},{10,14},{12... | collective-permute-start | bytes 393224 | tf_op jit(solution)/shard_map/ppermute | solution.py:98
  283.3 8.0 %collective-permute-start.12 = (bf16[128,512]{0,1:T(8,128)(2,1)S(1)}, bf16[128,512]{0,1:T(8,128)(2,1)S(1)}, u32[]{:S(2)}, u32[]{:S(2)}) collective-permute-start(bf16[128,512]{0,1:T(8,128)(2,1)S(1)} %get-tuple-element.56), channel_id=1, source_target_pairs={{0,6},{2,0},{4,2},{6,4},{1,7},{3,1},{5,3},{7,5},{8,14},{10,8},{12,... | collective-permute-start | bytes 393224 | tf_op jit(solution)/shard_map/ppermute | solution.py:98
Sparse Core Ops, SparseCore 0:
  10.1 79.3 all-gather.2
  115.6 68.1 all-gather.4
where the time goes:
time: 341 us; the launch traced here: 339 us
  waiting for transfers between devices  169 us (50%)
  starting transfers between devices  43 us (13%)
  other arithmetic  38.1 us (11%)
  blocking collectives  38 us (11%)
  local copies, waits for them, and re-layouts  23.5 us (7%)
  between operations  15.4 us (5%)
  matrix products  12.8 us (4%)
    all_gather x2, waiting for transfers between devices, gather_z(): return lax.all_gather(x, 'z', axis=0, tiled=True)  120 us
    psum x2, blocking collectives, local(): sums = lax.psum(sums, axis)  38 us
    concatenate x4, other arithmetic, swap_cat(): return jnp.concatenate([x, lax.ppermute(x, axis_name, [(0, 1), (1, 0)])], 0)  19.3 us
    ppermute x4, starting transfers between devices, swap_cat(): return jnp.concatenate([x, lax.ppermute(x, axis_name, [(0, 1), (1, 0)])], 0)  13.8 us
    ppermute x1, waiting for transfers between devices, reduce_scatter_head(): lax.ppermute(sent, 'xl', [(0, 1), (1, 0)]).astype(jnp.float32)  13.6 us
    ppermute x4, waiting for transfers between devices, swap_cat(): return jnp.concatenate([x, lax.ppermute(x, axis_name, [(0, 1), (1, 0)])], 0)  11.2 us
    ppermute x3, starting transfers between devices, reduce_scatter_head(): lax.ppermute(piece, 'y', [(i, (i + shift) % ny) for i in range(ny)])  10.4 us
    ppermute x3, waiting for transfers between devices, local(): lax.ppermute(jnp.take(quarters, me ^ flip, axis=1), pair, perm)  10.2 us
  transfers between devices with their start and end apart: 15, of which 10 were waited for; matrix products, arithmetic and copies ran while one was open for 6% of the time, Pallas kernels for 0%

commit v1 on v0

--- a/solution.py
+++ b/solution.py
@@ -16,6 +16,13 @@
 HEAD = ("y", "xl")
 
 
+def start_the_slabs(work_x, pos_dim):
+    earlier = jnp.concatenate(
+        lax.all_to_all(jnp.stack(lax.axis_size("z") * [work_x], axis=0), "z", 0, 0), pos_dim
+    )
+    return earlier
+
+
 def doc_layout(row_map, doc_lengths):
     doc_ends = jnp.cumsum(doc_lengths)
     doc_starts = doc_ends - doc_lengths
@@ -53,7 +60,7 @@
 
 
 def gather_z(x):
-    return lax.all_gather(x, "z", axis=0, tiled=True)
+    return start_the_slabs(x, 0)
 
 
 def gather_pair(x):

time: 341 us -> 381 us (1.12)
  waiting for transfers between devices: 169 us -> 193 us
  starting transfers between devices: 43 us -> 66.9 us
  between operations: 15.4 us -> 2.04 us
  blocking collectives: 38 us -> 42.4 us
    all_to_all x0 -> x2, waiting for transfers between devices: none -> 142 us  [start_the_slabs(): lax.all_to_all(jnp.stack(lax.axis_size('z') * [work_x], axis=0), 'z', 0, 0)]
    all_gather x2 -> x0, waiting for transfers between devices: 120 us -> none  [gather_z(): return lax.all_gather(x, 'z', axis=0, tiled=True)]
    all_to_all x0 -> x2, starting transfers between devices: none -> 22.9 us  [start_the_slabs(): lax.all_to_all(jnp.stack(lax.axis_size('z') * [work_x], axis=0), 'z', 0, 0)]
    psum x2, blocking collectives: 38 us -> 42.4 us  [local(): sums = lax.psum(sums, axis)]
  transfers between devices with their start and end apart: 15 -> 15, of which waited for: 10 -> 10; matrix products, arithmetic and copies ran while one was open for 6% -> 5% of each run, Pallas kernels for 0% -> 0%
where the time goes in v1:
time: 381 us; the launch traced here: 379 us
  waiting for transfers between devices  193 us (51%)
  starting transfers between devices  66.9 us (18%)
  blocking collectives  42.4 us (11%)
  other arithmetic  37.4 us (10%)
  local copies, waits for them, and re-layouts  24.8 us (7%)
  matrix products  12.8 us (3%)
    all_to_all x2, waiting for transfers between devices, start_the_slabs(): lax.all_to_all(jnp.stack(lax.axis_size('z') * [work_x], axis=0), 'z', 0, 0)  142 us
    psum x2, blocking collectives, local(): sums = lax.psum(sums, axis)  42.4 us
    all_to_all x2, starting transfers between devices, start_the_slabs(): lax.all_to_all(jnp.stack(lax.axis_size('z') * [work_x], axis=0), 'z', 0, 0)  22.9 us
    concatenate x4, other arithmetic, swap_cat(): return jnp.concatenate([x, lax.ppermute(x, axis_name, [(0, 1), (1, 0)])], 0)  19.3 us
    ppermute x4, waiting for transfers between devices, swap_cat(): return jnp.concatenate([x, lax.ppermute(x, axis_name, [(0, 1), (1, 0)])], 0)  14.5 us
    ppermute x4, starting transfers between devices, swap_cat(): return jnp.concatenate([x, lax.ppermute(x, axis_name, [(0, 1), (1, 0)])], 0)  14 us
    ppermute x1, waiting for transfers between devices, reduce_scatter_head(): lax.ppermute(sent, 'xl', [(0, 1), (1, 0)]).astype(jnp.float32)  13.1 us
    ppermute x3, starting transfers between devices, reduce_scatter_head(): lax.ppermute(piece, 'y', [(i, (i + shift) % ny) for i in range(ny)])  10.7 us
  transfers between devices with their start and end apart: 15, of which 10 were waited for; matrix products, arithmetic and copies ran while one was open for 5% of the time, Pallas kernels for 0%

profile of v1, /device:TPU:8, one launch (start us, length us, event | category | flops | bytes accessed | tf_op | source)
XLA Modules:
  0.0 379.2 jit_solution(14696119706966743005)
XLA Ops:
  1.6 1.8 stack.10
  3.3 15.4 %all-to-all-start = ((bf16[16,64,1280]{2,1,0:T(8,128)(2,1)}), bf16[16,64,1280]{2,1,0:T(8,128)(2,1)}, u32[]{:S(2)}, u32[]{:S(2)}) async-start(bf16[16,64,1280]{2,1,0:T(8,128)(2,1)} %stack.10), calls=%async_computation | async-start | bytes 5242880 | tf_op jit(solution)/shard_map/all_to_all | solution.py:21
  21.0 1.9 collective-permute-start
  22.9 4.9 %collective-permute-start.1 = (bf16[128,1024]{0,1:T(8,128)(2,1)S(1)}, bf16[128,1024]{0,1:T(8,128)(2,1)S(1)}, u32[]{:S(2)}, u32[]{:S(2)}) collective-permute-start(bf16[128,1024]{0,1:T(8,128)(2,1)S(1)} %get-tuple-element.58), channel_id=1, source_target_pairs={{0,16},{8,24},{16,0},{24,8},{1,17},{9,25},{17,1},{25,9},{2,18},{10... | collective-permute-start | bytes 786440 | tf_op jit(solution)/shard_map/ppermute | solution.py:139
  27.8 2.2 collective-permute-start.2
  30.1 5.3 %collective-permute-done.1 = bf16[128,1024]{0,1:T(8,128)(2,1)S(1)} collective-permute-done((bf16[128,1024]{0,1:T(8,128)(2,1)S(1)}, bf16[128,1024]{0,1:T(8,128)(2,1)S(1)}, u32[]{:S(2)}, u32[]{:S(2)}) %collective-permute-start.1) | collective-permute-done | bytes 262176 | tf_op jit(solution)/shard_map/ppermute | solution.py:139
  35.4 4.9 %collective-permute-done.2 = bf16[128,1024]{0,1:T(8,128)(2,1)} collective-permute-done((bf16[128,1024]{0,1:T(8,128)(2,1)S(1)}, bf16[128,1024]{0,1:T(8,128)(2,1)}, u32[]{:S(2)}, u32[]{:S(2)}) %collective-permute-start.2) | collective-permute-done | bytes 262176 | tf_op jit(solution)/shard_map/ppermute | solution.py:139
  40.3 96.2 %all-to-all-done = bf16[16,64,1280]{2,1,0:T(8,128)(2,1)} async-done(((bf16[16,64,1280]{2,1,0:T(8,128)(2,1)}), bf16[16,64,1280]{2,1,0:T(8,128)(2,1)}, u32[]{:S(2)}, u32[]{:S(2)}) %all-to-all-start) | async-done | bytes 2621472 | tf_op jit(solution)/shard_map/all_to_all | solution.py:21
  136.6 2.5 fusion.11
  139.2 1.9 collective-permute-start.3
  142.1 1.4 collective-permute-done.3
  144.6 4.9 %collective-permute-start.4 = (f32[128,768]{0,1:T(8,128)S(1)}, f32[128,768]{0,1:T(8,128)S(1)}, u32[]{:S(2)}, u32[]{:S(2)}) collective-permute-start(f32[128,768]{0,1:T(8,128)S(1)} %slice_add_fusion), channel_id=1, source_target_pairs={{0,16},{8,24},{16,0},{24,8},{1,17},{9,25},{17,1},{25,9},{2,18},{10... | collective-permute-start | bytes 1179656 | tf_op jit(solution)/shard_map/ppermute | solution.py:148
  149.7 9.4 %collective-permute-done.4 = f32[128,768]{0,1:T(8,128)S(1)} collective-permute-done((f32[128,768]{0,1:T(8,128)S(1)}, f32[128,768]{0,1:T(8,128)S(1)}, u32[]{:S(2)}, u32[]{:S(2)}) %collective-permute-start.4) | collective-permute-done | bytes 393248 | tf_op jit(solution)/shard_map/ppermute | solution.py:148
  162.0 1.1 stack.11
  163.0 7.5 %all-to-all-start.1 = ((bf16[16,136,256]{2,1,0:T(8,128)(2,1)}), bf16[16,136,256]{2,1,0:T(8,128)(2,1)S(1)}, u32[]{:S(2)}, u32[]{:S(2)}) async-start(bf16[16,136,256]{2,1,0:T(8,128)(2,1)} %stack.11), calls=%async_computation.1 | async-start | bytes 2228224 | tf_op jit(solution)/shard_map/all_to_all | solution.py:21
  170.6 1.3 slice.159
  171.9 4.9 %collective-permute-start.7 = (bf16[1024,512]{1,0:T(8,128)(2,1)S(1)}, bf16[1024,512]{1,0:T(8,128)(2,1)}, u32[]{:S(2)}, u32[]{:S(2)}) collective-permute-start(bf16[1024,512]{1,0:T(8,128)(2,1)S(1)} %slice.159), channel_id=1, source_target_pairs={{0,16},{16,0},{1,17},{17,1},{2,18},{18,2},{3,19},{19,3},{4,20},{20... | collective-permute-start | bytes 3145736 | tf_op jit(solution)/shard_map/ppermute | solution.py:59
  176.8 45.6 %all-to-all-done.1 = bf16[16,136,256]{2,1,0:T(8,128)(2,1)S(1)} async-done(((bf16[16,136,256]{2,1,0:T(8,128)(2,1)}), bf16[16,136,256]{2,1,0:T(8,128)(2,1)S(1)}, u32[]{:S(2)}, u32[]{:S(2)}) %all-to-all-start.1) | async-done | bytes 1114144 | tf_op jit(solution)/shard_map/all_to_all | solution.py:21
  222.4 4.9 %collective-permute-start.5 = (bf16[2176,256]{1,0:T(8,128)(2,1)S(1)}, bf16[2176,256]{1,0:T(8,128)(2,1)S(1)}, u32[]{:S(2)}, u32[]{:S(2)}) collective-permute-start(bf16[2176,256]{1,0:T(8,128)(2,1)S(1)} %bitcast.114), channel_id=1, source_target_pairs={{0,16},{16,0},{1,17},{17,1},{2,18},{18,2},{3,19},{19,3},{4,20},{20... | collective-permute-start | bytes 3342344 | tf_op jit(solution)/shard_map/ppermute | solution.py:59
  227.3 2.7 pad_maximum_fusion.3
  230.0 2.0 collective-permute-start.8
  232.1 14.5 %collective-permute-done.5 = bf16[2176,256]{1,0:T(8,128)(2,1)S(1)} collective-permute-done((bf16[2176,256]{1,0:T(8,128)(2,1)S(1)}, bf16[2176,256]{1,0:T(8,128)(2,1)S(1)}, u32[]{:S(2)}, u32[]{:S(2)}) %collective-permute-start.5) | collective-permute-done | bytes 1114144 | tf_op jit(solution)/shard_map/ppermute | solution.py:59
  246.6 1.7 pad_maximum_fusion.2
  248.4 2.1 collective-permute-start.6
  252.3 1.4 subtract_convert_fusion
  256.3 3.6 pad_maximum_fusion.1
  259.9 11.3 %pad_maximum_fusion = bf16[8704,256]{1,0:T(8,128)(2,1)S(1)} fusion(bf16[4352,256]{1,0:T(8,128)(2,1)} %collective-permute-done.6, bf16[2176,256]{1,0:T(8,128)(2,1)S(1)} %copy-done.1, bf16[2176,256]{1,0:T(8,128)(2,1)S(1)} %bitcast.116), kind=kLoop, calls=%fused_computation.13 | loop fusion | flops 13369344 | bytes 8912896 | tf_op jit(solution)/shard_map/concatenate | solution.py:59
  271.2 2.5 slice.153
  274.1 1.2 scatter_custom_fusion
  275.3 1.2 gather_fusion
  277.3 2.9 gather_fusion.2
  280.6 4.5 %fusion.63 = (f32[2,4,64]{2,1,0:T(4,128)S(1)}, bf16[2,4,64,2112]{3,2,1,0:T(8,128)(2,1)}) fusion(pred[2,64,2112]{2,1,0:T(8,128)(4,1)S(1)} %compare_and_fusion, bf16[2,2112,256]{2,1,0:T(8,128)(2,1)S(1)} %bitcast.122, bf16[2,64,4,64]{3,1,2,0:T(8,128)(2,1)} %copy.77, bf16[2,64,4,64]{3,1,2,0:T(8,128)(2,1)} %copy.76), kind=kOutput, calls=%fused_computation.145 | convolution fusion | flops 283576384 | bytes 3934208 | tf_op jit(solution)/shard_map/sub | solution.py:194
  285.1 2.4 fusion.19
  287.7 3.4 fusion.40
  291.1 2.0 gather_fusion.3
  293.1 3.3 select_bitcast_fusion.1
  296.5 2.3 gather_fusion.4
  300.2 3.4 collective-permute-start.9
  303.7 13.1 %collective-permute-done.9 = bf16[128,4,512]{0,2,1:T(8,128)(2,1)} collective-permute-done((bf16[128,4,512]{0,2,1:T(8,128)(2,1)}, bf16[128,4,512]{0,2,1:T(8,128)(2,1)}, u32[]{:S(2)}, u32[]{:S(2)}) %collective-permute-start.9) | collective-permute-done | bytes 524320 | tf_op jit(solution)/shard_map/ppermute | solution.py:101
  316.8 1.1 fusion.30
  319.0 3.5 collective-permute-start.10
  322.5 2.8 collective-permute-start.11
  325.3 4.3 %collective-permute-start.12 = (bf16[128,512]{0,1:T(8,128)(2,1)S(1)}, bf16[128,512]{0,1:T(8,128)(2,1)S(1)}, u32[]{:S(2)}, u32[]{:S(2)}) collective-permute-start(bf16[128,512]{0,1:T(8,128)(2,1)S(1)} %get-tuple-element.54), channel_id=1, source_target_pairs={{0,6},{2,0},{4,2},{6,4},{1,7},{3,1},{5,3},{7,5},{8,14},{10,8},{12,... | collective-permute-start | bytes 393224 | tf_op jit(solution)/shard_map/ppermute | solution.py:105
  331.9 1.6 collective-permute-done.12
  333.5 1.2 fusion.32
  334.7 9.2 %psum.14 = f32[2,512]{1,0:T(2,128)S(1)} all-reduce(f32[2,512]{1,0:T(2,128)S(1)} %pad_maximum_fusion.12), channel_id=1, replica_groups=mesh['z'=16,'xh'=2,'c'=2,'y'=4,'xl'=2] {'xh','c'}, use_global_device_ids=true, to_apply=%region_11.15 | all-reduce | flops 1024 | bytes 8192 | tf_op jit(solution)/shard_map/psum | solution.py:224
  343.9 33.3 %psum.15 = f32[2,512]{1,0:T(2,128)S(1)} all-reduce(f32[2,512]{1,0:T(2,128)S(1)} %psum.14), channel_id=1, replica_groups=mesh['z'=16,'xh'=2,'c'=2,'y'=4,'xl'=2] {'z'}, use_global_device_ids=true, to_apply=%region_12.16 | all-reduce | flops 1024 | bytes 8192 | tf_op jit(solution)/shard_map/psum | solution.py:224
  378.0 1.3 divide_subtract_fusion
  (99 shorter events, 19.0 us)
Async XLA Ops:
  3.3 15.4 %copy-start.4 = (bf16[128,4096]{1,0:T(8,128)(2,1)S(1)}, bf16[128,4096]{1,0:T(8,128)(2,1)}, u32[]{:S(2)}) copy-start(bf16[128,4096]{1,0:T(8,128)(2,1)} %param.15) | copy-start | bytes 3145732
  3.3 133.2 %all-to-all-start = ((bf16[16,64,1280]{2,1,0:T(8,128)(2,1)}), bf16[16,64,1280]{2,1,0:T(8,128)(2,1)}, u32[]{:S(2)}, u32[]{:S(2)}) async-start(bf16[16,64,1280]{2,1,0:T(8,128)(2,1)} %stack.10), calls=%async_computation | async-start | bytes 5242880 | tf_op jit(solution)/shard_map/all_to_all | solution.py:21
  18.7 1.3 copy-start.5
  21.0 9.1 %collective-permute-start = (bf16[128,1024]{0,1:T(8,128)(2,1)S(1)}, bf16[128,1024]{0,1:T(8,128)(2,1)S(1)}, u32[]{:S(2)}, u32[]{:S(2)}) collective-permute-start(bf16[128,1024]{0,1:T(8,128)(2,1)S(1)} %get-tuple-element.59), channel_id=1, source_target_pairs={{0,8},{8,0},{16,24},{24,16},{1,9},{9,1},{17,25},{25,17},{2,10},{10... | collective-permute-start | bytes 786440 | tf_op jit(solution)/shard_map/ppermute | solution.py:139
  22.9 12.5 %collective-permute-start.1 = (bf16[128,1024]{0,1:T(8,128)(2,1)S(1)}, bf16[128,1024]{0,1:T(8,128)(2,1)S(1)}, u32[]{:S(2)}, u32[]{:S(2)}) collective-permute-start(bf16[128,1024]{0,1:T(8,128)(2,1)S(1)} %get-tuple-element.58), channel_id=1, source_target_pairs={{0,16},{8,24},{16,0},{24,8},{1,17},{9,25},{17,1},{25,9},{2,18},{10... | collective-permute-start | bytes 786440 | tf_op jit(solution)/shard_map/ppermute | solution.py:139
  27.8 12.5 %collective-permute-start.2 = (bf16[128,1024]{0,1:T(8,128)(2,1)S(1)}, bf16[128,1024]{0,1:T(8,128)(2,1)}, u32[]{:S(2)}, u32[]{:S(2)}) collective-permute-start(bf16[128,1024]{0,1:T(8,128)(2,1)S(1)} %get-tuple-element.57), channel_id=1, source_target_pairs={{0,24},{8,16},{16,8},{24,0},{1,25},{9,17},{17,9},{25,1},{2,26},{10... | collective-permute-start | bytes 786440 | tf_op jit(solution)/shard_map/ppermute | solution.py:139
  139.1 2.1 copy-start.8
  139.1 2.3 copy-start.9
  139.2 4.3 %collective-permute-start.3 = (f32[256,768]{0,1:T(8,128)S(1)}, f32[256,768]{0,1:T(8,128)}, u32[]{:S(2)}, u32[]{:S(2)}) collective-permute-start(f32[256,768]{0,1:T(8,128)S(1)} %pad_maximum_fusion.4), channel_id=1, source_target_pairs={{0,8},{8,0},{16,24},{24,16},{1,9},{9,1},{17,25},{25,17},{2,10},{10... | collective-permute-start | bytes 2359304 | tf_op jit(solution)/shard_map/ppermute | solution.py:145
  144.6 14.6 %collective-permute-start.4 = (f32[128,768]{0,1:T(8,128)S(1)}, f32[128,768]{0,1:T(8,128)S(1)}, u32[]{:S(2)}, u32[]{:S(2)}) collective-permute-start(f32[128,768]{0,1:T(8,128)S(1)} %slice_add_fusion), channel_id=1, source_target_pairs={{0,16},{8,24},{16,0},{24,8},{1,17},{9,25},{17,1},{25,9},{2,18},{10... | collective-permute-start | bytes 1179656 | tf_op jit(solution)/shard_map/ppermute | solution.py:148
  160.3 0.8 copy-start.3
  163.0 59.3 %all-to-all-start.1 = ((bf16[16,136,256]{2,1,0:T(8,128)(2,1)}), bf16[16,136,256]{2,1,0:T(8,128)(2,1)S(1)}, u32[]{:S(2)}, u32[]{:S(2)}) async-start(bf16[16,136,256]{2,1,0:T(8,128)(2,1)} %stack.11), calls=%async_computation.1 | async-start | bytes 2228224 | tf_op jit(solution)/shard_map/all_to_all | solution.py:21
  171.9 55.5 %collective-permute-start.7 = (bf16[1024,512]{1,0:T(8,128)(2,1)S(1)}, bf16[1024,512]{1,0:T(8,128)(2,1)}, u32[]{:S(2)}, u32[]{:S(2)}) collective-permute-start(bf16[1024,512]{1,0:T(8,128)(2,1)S(1)} %slice.159), channel_id=1, source_target_pairs={{0,16},{16,0},{1,17},{17,1},{2,18},{18,2},{3,19},{19,3},{4,20},{20... | collective-permute-start | bytes 3145736 | tf_op jit(solution)/shard_map/ppermute | solution.py:59
  222.4 24.2 %collective-permute-start.5 = (bf16[2176,256]{1,0:T(8,128)(2,1)S(1)}, bf16[2176,256]{1,0:T(8,128)(2,1)S(1)}, u32[]{:S(2)}, u32[]{:S(2)}) collective-permute-start(bf16[2176,256]{1,0:T(8,128)(2,1)S(1)} %bitcast.114), channel_id=1, source_target_pairs={{0,16},{16,0},{1,17},{17,1},{2,18},{18,2},{3,19},{19,3},{4,20},{20... | collective-permute-start | bytes 3342344 | tf_op jit(solution)/shard_map/ppermute | solution.py:59
  230.0 22.2 %slice-start = ((f32[128,768]{0,1:T(8,128)}), f32[128,512]{0,1:T(8,128)S(1)}, s32[]{:S(2)}) async-start(f32[128,768]{0,1:T(8,128)} %copy-done.3), calls=%async_computation.2 | async-start | bytes 524288 | tf_op jit(solution)/shard_map/slice | solution.py:150
  230.0 26.3 %collective-permute-start.8 = (bf16[2048,512]{1,0:T(8,128)(2,1)}, bf16[2048,512]{1,0:T(8,128)(2,1)}, u32[]{:S(2)}, u32[]{:S(2)}) collective-permute-start(bf16[2048,512]{1,0:T(8,128)(2,1)} %pad_maximum_fusion.3), channel_id=1, source_target_pairs={{0,8},{8,0},{1,9},{9,1},{2,10},{10,2},{3,11},{11,3},{4,12},{12,4},... | collective-permute-start | bytes 6291464 | tf_op jit(solution)/shard_map/ppermute | solution.py:59
  246.6 1.8 copy-start
  248.4 11.6 %collective-permute-start.6 = (bf16[4352,256]{1,0:T(8,128)(2,1)}, bf16[4352,256]{1,0:T(8,128)(2,1)}, u32[]{:S(2)}, u32[]{:S(2)}) collective-permute-start(bf16[4352,256]{1,0:T(8,128)(2,1)} %pad_maximum_fusion.2), channel_id=1, source_target_pairs={{0,8},{8,0},{1,9},{9,1},{2,10},{10,2},{3,11},{11,3},{4,12},{12,4},... | collective-permute-start | bytes 6684680 | tf_op jit(solution)/shard_map/ppermute | solution.py:59
  256.3 3.6 copy-start.1
  277.3 3.0 copy-start.12
  291.1 2.0 copy-start.7
  296.5 2.3 copy-start.6
  299.3 30.4 %copy-start.13 = (s32[32]{0:T(128)S(1)}, s32[32]{0:T(128)}, u32[]{:S(2)}) copy-start(s32[32]{0:T(128)} %param.23) | copy-start | bytes 388
  299.3 31.7 %copy-start.10 = (s32[128]{0:T(128)S(1)}, s32[128]{0:T(128)}, u32[]{:S(2)}) copy-start(s32[128]{0:T(128)} %param.21) | copy-start | bytes 1540
  299.3 31.7 %copy-start.11 = (s32[32]{0:T(128)S(1)}, s32[32]{0:T(128)}, u32[]{:S(2)}) copy-start(s32[32]{0:T(128)} %get-tuple-element.74) | copy-start | bytes 388
  300.2 16.5 %collective-permute-start.9 = (bf16[128,4,512]{0,2,1:T(8,128)(2,1)}, bf16[128,4,512]{0,2,1:T(8,128)(2,1)}, u32[]{:S(2)}, u32[]{:S(2)}) collective-permute-start(bf16[128,4,512]{0,2,1:T(8,128)(2,1)} %bitcast_convert_fusion), channel_id=1, source_target_pairs={{0,1},{1,0},{2,3},{3,2},{4,5},{5,4},{6,7},{7,6},{8,9},{9,8},{10,11... | collective-permute-start | bytes 1572872 | tf_op jit(solution)/shard_map/ppermute | solution.py:101
  317.9 1.0 copy-start.2
  319.0 12.2 %collective-permute-start.10 = (bf16[128,512]{0,1:T(8,128)(2,1)S(1)}, bf16[128,512]{0,1:T(8,128)(2,1)S(1)}, u32[]{:S(2)}, u32[]{:S(2)}) collective-permute-start(bf16[128,512]{0,1:T(8,128)(2,1)S(1)} %get-tuple-element.53), channel_id=1, source_target_pairs={{0,2},{2,4},{4,6},{6,0},{1,3},{3,5},{5,7},{7,1},{8,10},{10,12},{12... | collective-permute-start | bytes 393224 | tf_op jit(solution)/shard_map/ppermute | solution.py:105
  322.5 9.5 %collective-permute-start.11 = (bf16[128,512]{0,1:T(8,128)(2,1)S(1)}, bf16[128,512]{0,1:T(8,128)(2,1)S(1)}, u32[]{:S(2)}, u32[]{:S(2)}) collective-permute-start(bf16[128,512]{0,1:T(8,128)(2,1)S(1)} %get-tuple-element.55), channel_id=1, source_target_pairs={{0,4},{2,6},{4,0},{6,2},{1,5},{3,7},{5,1},{7,3},{8,12},{10,14},{12... | collective-permute-start | bytes 393224 | tf_op jit(solution)/shard_map/ppermute | solution.py:105
  325.3 8.2 %collective-permute-start.12 = (bf16[128,512]{0,1:T(8,128)(2,1)S(1)}, bf16[128,512]{0,1:T(8,128)(2,1)S(1)}, u32[]{:S(2)}, u32[]{:S(2)}) collective-permute-start(bf16[128,512]{0,1:T(8,128)(2,1)S(1)} %get-tuple-element.54), channel_id=1, source_target_pairs={{0,6},{2,0},{4,2},{6,4},{1,7},{3,1},{5,3},{7,5},{8,14},{10,8},{12,... | collective-permute-start | bytes 393224 | tf_op jit(solution)/shard_map/ppermute | solution.py:105
